TPU v7x, 32 devices: a whole 2x2x4 slice. The times are simulated.
32 devices in a mesh: task: 2 (over y), row: 4 (over z), col: 4 (over x, core).
Axes of the slice: x: 2, y: 2, z: 4, core: 2. Of those that a mesh axis runs over, the one named last changes fastest.
Arguments:
- features: bfloat16 [164, 4096], P(None, ('task', 'row', 'col')), parts along dimension 1, may hold values from -6 to 6
- rung_index: int32 [4096], P(('task', 'row', 'col')), parts along dimension 0, may hold values from 0 to 3
- w_first: bfloat16 [164, 512], replicated, may hold values from -0.5 to 0.5
- b_first: float32 [512], replicated, may hold values from -4 to 4
- w_second: bfloat16 [512, 512], replicated, may hold values from -0.25 to 0.25
- b_second: float32 [512], replicated, may hold values from -4 to 4
- w_third: bfloat16 [512, 64], replicated, may hold values from -0.25 to 0.25
- targets: float32 [16, 4096], P(None, ('task', 'row', 'col')), parts along dimension 1, may hold values from -80 to 80
- fidelity_factor: float32 [8, 4], P('task'), parts along dimension 0, may hold values from -4 to 4
- inverse_scale: float32 [2], P('task'), parts along dimension 0, may hold values from 0.02 to 0.1
- noise_var: float32 [2], P('task'), parts along dimension 0, may hold values from 0.3 to 1
Outputs:
- solution: float32 [16, 4096], P(None, ('task', 'row', 'col')), parts along dimension 1
- residual: float32 [16, 4096], P(None, ('task', 'row', 'col')), parts along dimension 1
There are 2 independent parts, one for each index of `task`. A program takes and returns all parts, laid end to end along the dimension named above; an argument that names none is the same for every part. Nothing has to cross between parts.
All inputs are finite; a program needn't handle non-finite values.
Results may differ from a plain program's by a relative error of at most 0.012.
The roundings to bfloat16 on the way count: a program that leaves them out, or rounds other values in their place, can miss the bound.
Values may be sent and summed in bfloat16 or wider, within the bound.
No kernel may reach another device: no remote copies, remote signals or barrier semaphores. Data moves between devices by JAX's collectives and lax.ppermute only.
A program may use at most 64 MiB of HBM per device.

v0:
```python
import jax
import jax.numpy as jnp
from jax import lax
from jax.sharding import PartitionSpec as P

ITERS = 2


def fidelity_matrix(fidelity_factor):
    lower = jnp.tril(fidelity_factor)
    return jnp.dot(lower, lower.T, precision=lax.Precision.HIGHEST) + 0.5 * jnp.eye(
        fidelity_factor.shape[0], dtype=jnp.float32
    )


def left_product(weights, values):
    return lax.dot_general(
        weights, values, (((0,), (0,)), ((), ())), preferred_element_type=jnp.float32
    )


def outer_gram(left_side, right_side):
    return lax.dot_general(
        left_side, right_side, (((1,), (1,)), ((), ())), precision=lax.Precision.HIGHEST
    )


def solve_spd(matrix, right_side):
    return jax.scipy.linalg.cho_solve((jnp.linalg.cholesky(matrix), True), right_side)


def block_size(total_count, largest):
    chosen = min(total_count, largest)
    while total_count % chosen != 0:
        chosen = chosen - 1
    return chosen


def rung_fidelity(fidelity, rung_value):
    levels = jnp.arange(fidelity.shape[0], dtype=jnp.float32)
    onehot = (rung_value.astype(jnp.float32)[None, :] == levels[:, None]).astype(jnp.float32)
    return jnp.dot(fidelity, onehot, precision=lax.Precision.HIGHEST)


def kernel_image(embedding, squares, rung_value, col_fidelity, inverse_scale, direction):
    count = embedding.shape[1]
    row_block = block_size(count, 2048)
    col_block = block_size(count, 2048)
    levels = jnp.arange(col_fidelity.shape[0], dtype=jnp.float32)

    def one_row_block(block_number):
        first_row = block_number * row_block
        rows_embedding = lax.dynamic_slice_in_dim(embedding, first_row, row_block, 1)
        rows_squares = lax.dynamic_slice_in_dim(squares, first_row, row_block, 0)
        rows_rung = lax.dynamic_slice_in_dim(rung_value, first_row, row_block, 0)
        rows_match = rows_rung.astype(jnp.float32)[:, None] == levels[None, :]

        def one_col_block(running, column_number):
            first_col = column_number * col_block
            cols_embedding = lax.dynamic_slice_in_dim(embedding, first_col, col_block, 1)
            cols_squares = lax.dynamic_slice_in_dim(squares, first_col, col_block, 0)
            cols_fidelity = lax.dynamic_slice_in_dim(col_fidelity, first_col, col_block, 1)
            cols_direction = lax.dynamic_slice_in_dim(direction, first_col, col_block, 1)
            inner = left_product(rows_embedding, cols_embedding)
            distance = rows_squares[:, None] + cols_squares[None, :] - 2.0 * inner
            tile_fidelity = cols_fidelity[0][None, :]
            for level in range(1, col_fidelity.shape[0]):
                tile_fidelity = jnp.where(
                    rows_match[:, level : level + 1], cols_fidelity[level][None, :], tile_fidelity
                )
            kernel = jnp.exp(-inverse_scale[0] * distance) * tile_fidelity
            contribution = lax.dot_general(
                cols_direction, kernel, (((1,), (1,)), ((), ())), precision=lax.Precision.HIGHEST
            )
            return (running + contribution, None)

        start_value = jnp.zeros((direction.shape[0], row_block), jnp.float32)
        result, unused = lax.scan(
            one_col_block, start_value, jnp.arange(count // col_block, dtype=jnp.int32)
        )
        return result

    stacked = lax.map(one_row_block, jnp.arange(count // row_block, dtype=jnp.int32))
    return jnp.transpose(stacked, (1, 0, 2)).reshape(direction.shape[0], count)


def on_device(
    features,
    rung_index,
    w_first,
    b_first,
    w_second,
    b_second,
    w_third,
    targets,
    fidelity_factor,
    inverse_scale,
    noise_var,
):
    fidelity = fidelity_matrix(fidelity_factor)
    hidden_one = jax.nn.silu(left_product(w_first, features) + b_first[:, None]).astype(
        jnp.bfloat16
    )
    hidden_two = jax.nn.silu(left_product(w_second, hidden_one) + b_second[:, None]).astype(
        jnp.bfloat16
    )
    embedding = left_product(w_third, hidden_two).astype(jnp.bfloat16)
    rung_value = rung_index.astype(jnp.float32).astype(jnp.bfloat16)
    own_count = targets.shape[1]
    own_first = (lax.axis_index("row") * lax.axis_size("col") + lax.axis_index("col")) * own_count
    all_embedding = lax.all_gather(embedding, ("row", "col"), axis=1, tiled=True)
    all_rung = lax.all_gather(rung_value, ("row", "col"), axis=0, tiled=True)
    all_targets = lax.all_gather(targets, ("row", "col"), axis=1, tiled=True)
    squares = jnp.sum(jnp.square(all_embedding.astype(jnp.float32)), axis=0)
    col_fidelity = rung_fidelity(fidelity, all_rung)
    solution = jnp.zeros_like(all_targets)
    residual = all_targets
    direction = all_targets
    gram = outer_gram(residual, residual)
    for iteration in range(ITERS):
        image = (
            kernel_image(all_embedding, squares, all_rung, col_fidelity, inverse_scale, direction)
            + noise_var[0] * direction
        )
        curvature = outer_gram(direction, image)
        step_matrix = solve_spd(curvature, gram)
        solution = solution + jnp.dot(step_matrix.T, direction, precision=lax.Precision.HIGHEST)
        residual = residual - jnp.dot(step_matrix.T, image, precision=lax.Precision.HIGHEST)
        if iteration + 1 < ITERS:
            new_gram = outer_gram(residual, residual)
            update_matrix = solve_spd(gram, new_gram)
            direction = residual + jnp.dot(
                update_matrix.T, direction, precision=lax.Precision.HIGHEST
            )
            gram = new_gram
    own_solution = lax.dynamic_slice_in_dim(solution, own_first, own_count, 1)
    own_residual = lax.dynamic_slice_in_dim(residual, own_first, own_count, 1)
    return (own_solution, own_residual)


def solution(mesh):
    placed = (
        P(None, ("task", "row", "col")),
        P(("task", "row", "col")),
        P(),
        P(),
        P(),
        P(),
        P(),
        P(None, ("task", "row", "col")),
        P("task", None),
        P("task"),
        P("task"),
    )
    return jax.shard_map(
        on_device,
        mesh=mesh,
        in_specs=placed,
        out_specs=(P(None, ("task", "row", "col")), P(None, ("task", "row", "col"))),
        check_vma=False,
    )
```

profile of v0, /device:TPU:0, one launch (start us, length us, event | category | flops | bytes accessed | tf_op | source)
XLA Modules:
  0.0 122.0 jit_solution(9418712131245514869)
XLA Ops:
  0.6 0.7 convert_bitcast_fusion
  1.4 23.1 %all-gather = bf16[16,1,128]{2,1,0:T(2,128)(2,1)S(1)} all-gather(bf16[1,1,128]{2,1,0:T(2,128)(2,1)S(1)} %convert_bitcast_fusion), channel_id=1, replica_groups=mesh['task'=2,'row'=4,'col'=4] {'row','col'}, dimensions={0}, use_global_device_ids=true | all-gather | bytes 4352 | tf_op jit(solution)/shard_map/all_gather | solution.py:112
  24.5 0.9 convolution_add_fusion.4
  25.7 1.3 %multiply_convert_fusion.1 = bf16[512,128]{1,0:T(8,128)(2,1)S(1)} fusion(bf16[164,512]{1,0:T(8,128)(2,1)} %param.16, bf16[164,128]{1,0:T(8,128)(2,1)} %param.14, f32[512]{0:T(512)} %param.17), kind=kOutput, calls=%fused_computation.14 | convolution fusion | flops 21889024 | bytes 343040 | tf_op jit(solution)/shard_map/dot_general | solution.py:17
  26.9 1.4 %fusion.2 = bf16[64,128]{1,0:T(8,128)(2,1)S(1)} fusion(bf16[512,64]{0,1:T(8,128)(2,1)} %param.20, bf16[512,128]{1,0:T(8,128)(2,1)S(1)} %multiply_convert_fusion.1, bf16[512,512]{1,0:T(8,128)(2,1)S(1)} %copy-done, f32[512]{0:T(512)} %param.19), kind=kOutput, calls=%fused_computation.10 | convolution fusion | flops 75898880 | bytes 739328 | tf_op jit(solution)/shard_map/dot_general | solution.py:17
  28.3 18.2 %all_gather.9 = bf16[64,2048]{1,0:T(8,128)(2,1)S(1)} all-gather(bf16[64,128]{1,0:T(8,128)(2,1)S(1)} %fusion.2), channel_id=1, replica_groups=mesh['task'=2,'row'=4,'col'=4] {'row','col'}, dimensions={1}, use_global_device_ids=true | all-gather | bytes 278528 | tf_op jit(solution)/shard_map/all_gather | solution.py:111
  47.2 6.6 %select_multiply_fusion = f32[2048,2048]{1,0:T(8,128)S(1)} fusion(bf16[64,2048]{1,0:T(8,128)(2,1)S(1)} %all_gather.9, f32[2048]{0:T(1024)S(1)} %bitcast.95, f32[2048]{0:T(1024)S(1)} %bitcast.96, f32[2048]{0:T(1024)S(1)} %bitcast.97, f32[2048]{0:T(1024)S(1)} %bitcast.94, f32[2048]{0:T(1024)S(1)} %multiply_reduce_fusion, f32[]{:T(128)} %bitcast, ...), kind=kOutput, calls=%fused_computation | convolution fusion | flops 570425344 | bytes 17086468 | tf_op jit(solution)/shard_map/while/body/eval_jaxpr/while/body/eval_jaxpr/dot_general | solution.py:17
  53.8 19.3 %all_gather.11 = f32[16,2048]{1,0:T(8,128)S(1)} all-gather(f32[16,128]{1,0:T(8,128)S(1)} %copy-done.2), channel_id=1, replica_groups=mesh['task'=2,'row'=4,'col'=4] {'row','col'}, dimensions={1}, use_global_device_ids=true | all-gather | bytes 139264 | tf_op jit(solution)/shard_map/all_gather | solution.py:113
  73.8 14.1 %fusion = f32[16,2048]{1,0:T(8,128)S(1)} fusion(f32[2048,2048]{1,0:T(8,128)S(1)} %select_multiply_fusion, f32[16,2048]{1,0:T(8,128)S(1)} %all_gather.11, f32[]{:T(128)} %bitcast.89), kind=kOutput, calls=%fused_computation.5 | convolution fusion | flops 805371904 | bytes 17039364 | tf_op jit(solution)/shard_map/while/body/eval_jaxpr/while/body/eval_jaxpr/dot_general | solution.py:72
  88.2 1.5 %cholesky.59 = f32[16,16]{1,0:T(8,128)S(1)} custom-call(f32[16,16]{1,0:T(8,128)S(1)} %add_multiply_fusion), custom_call_target="Cholesky" | custom-call | tf_op jit(solution)/shard_map/jit(cholesky)/cholesky | solution.py:29
  89.8 0.6 compare_reduce_fusion.2
  90.4 0.6 fusion.7
  91.1 1.2 %custom-call.9 = f32[1,16,16]{1,2,0:T(8,128)S(1)} custom-call(f32[1,16,16]{2,1,0:T(8,128)S(1)} %fusion.7), custom_call_target="InvertDiagBlocksLowerTriangular" | custom-call | tf_op jit(solution)/shard_map/jit(_cho_solve)/triangular_solve | solution.py:29
  92.3 0.2 fusion.30
  92.5 0.3 fusion.22
  93.0 0.3 convolution_subtract_fusion
  93.3 0.4 fusion.32
  93.8 1.5 %cholesky.70 = f32[16,16]{1,0:T(8,128)S(1)} custom-call(f32[16,16]{1,0:T(8,128)S(1)} %fusion.19), custom_call_target="Cholesky" | custom-call | tf_op jit(solution)/shard_map/jit(cholesky)/cholesky | solution.py:29
  95.4 0.6 compare_reduce_fusion.1
  96.0 0.6 fusion.8
  96.7 1.2 %custom-call.10 = f32[1,16,16]{1,2,0:T(8,128)S(1)} custom-call(f32[1,16,16]{2,1,0:T(8,128)S(1)} %fusion.8), custom_call_target="InvertDiagBlocksLowerTriangular" | custom-call | tf_op jit(solution)/shard_map/jit(_cho_solve)/triangular_solve | solution.py:29
  98.2 0.3 convolution_add_fusion
  98.6 17.1 %convolution_add_fusion.1 = f32[16,2048]{1,0:T(8,128)S(1)} fusion(f32[16,2048]{1,0:T(8,128)S(1)} %convolution_add_fusion, f32[2048,2048]{1,0:T(8,128)} %copy-done.1, f32[]{:T(128)} %bitcast.90), kind=kOutput, calls=%fused_computation.3 | convolution fusion | flops 805371904 | bytes 17039364 | tf_op jit(solution)/shard_map/while/body/eval_jaxpr/while/body/eval_jaxpr/dot_general | solution.py:72
  115.7 0.2 fusion.33
  116.0 1.5 %cholesky.81 = f32[16,16]{1,0:T(8,128)S(1)} custom-call(f32[16,16]{1,0:T(8,128)S(1)} %fusion.14), custom_call_target="Cholesky" | custom-call | tf_op jit(solution)/shard_map/jit(cholesky)/cholesky | solution.py:29
  117.5 0.6 compare_reduce_fusion
  118.2 0.6 fusion.9
  118.9 1.2 %custom-call.11 = f32[1,16,16]{1,2,0:T(8,128)S(1)} custom-call(f32[1,16,16]{2,1,0:T(8,128)S(1)} %fusion.9), custom_call_target="InvertDiagBlocksLowerTriangular" | custom-call | tf_op jit(solution)/shard_map/jit(_cho_solve)/triangular_solve | solution.py:29
  120.4 0.3 fusion.34
  120.8 0.3 fusion.35
  121.1 0.3 fusion.31
  121.4 0.6 dynamic-slice_subtract_fusion
  (27 shorter events, 1.8 us)
Async XLA Ops:
  0.6 26.3 %copy-start = (bf16[512,512]{1,0:T(8,128)(2,1)S(1)}, bf16[512,512]{1,0:T(8,128)(2,1)}, u32[]{:S(2)}) copy-start(bf16[512,512]{1,0:T(8,128)(2,1)} %param.18) | copy-start | bytes 1572868
  47.2 6.6 %copy-start.2 = (f32[16,128]{1,0:T(8,128)S(1)}, f32[16,128]{1,0:T(8,128)}, u32[]{:S(2)}) copy-start(f32[16,128]{1,0:T(8,128)} %param.21) | copy-start | bytes 24580
  53.8 20.0 %copy-start.1 = (f32[2048,2048]{1,0:T(8,128)}, f32[2048,2048]{1,0:T(8,128)S(1)}, u32[]{:S(2)}) copy-start(f32[2048,2048]{1,0:T(8,128)S(1)} %select_multiply_fusion) | copy-start | bytes 50331652
where the time goes:
time: 122 us
  blocking collectives  60.5 us (50%)
  matrix products  45.3 us (37%)
  other arithmetic  13.7 us (11%)
  between operations  2.14 us (2%)
    dot_general x2, matrix products, one_col_block(): lax.dot_general(cols_direction, kernel, (((1,), (1,)), ((), ())), precisi...  31.2 us
    all_gather x1, blocking collectives, on_device(): all_rung = lax.all_gather(rung_value, ('row', 'col'), axis=0, tiled=True)  23.1 us
    all_gather x1, blocking collectives, on_device(): all_targets = lax.all_gather(targets, ('row', 'col'), axis=1, tiled=True)  19.3 us
    all_gather x1, blocking collectives, on_device(): lax.all_gather(embedding, ('row', 'col'), axis=1, tiled=True)  18.2 us
    dot_general x3, matrix products, left_product(): lax.dot_general(weights, values, (((0,), (0,)), ((), ())), preferred_elem...  9.19 us
    another operation x9, other arithmetic, solve_spd(): jnp.linalg.cholesky(matrix)  6.57 us
    another operation x6, other arithmetic, solve_spd(): jax.scipy.linalg.cho_solve((jnp.linalg.cholesky(matrix), True), right_side)  5.63 us

commit v1 on v0

--- a/solution.py
+++ b/solution.py
@@ -4,6 +4,31 @@
 from jax.sharding import PartitionSpec as P
 
 ITERS = 2
+
+
+def open_sections_for(body, k_dim):
+    body = jnp.moveaxis(body, 0, k_dim)
+    g_now = body.shape
+    return body.reshape(*g_now[:k_dim], g_now[k_dim] * g_now[k_dim + 1], *g_now[k_dim + 2 :])
+
+
+def watch_the_racks(z_in, mesh_ax):
+    num = jax.lax.psum(1, axis_name=mesh_ax)
+    oldest = z_in[None]
+    for idx in range(num.bit_length() - 1):
+        taken_in = 1 << idx
+        v1 = tuple(((dev_j, dev_j ^ taken_in) for dev_j in range(num)))
+        t_next = jax.lax.ppermute(oldest, axis_name=mesh_ax, perm=v1)
+        long_array = jnp.stack([oldest, t_next])
+        heard = jax.lax.axis_index(mesh_ax)
+        upper = heard >> idx & 1
+        oldest = jnp.where(upper == 0, long_array, long_array[::-1]).reshape(-1, *z_in.shape)
+    return oldest
+
+
+def _hold_streams(u, own_rows, where_dim):
+    block_out = watch_the_racks(u, own_rows)
+    return open_sections_for(block_out, where_dim)
 
 
 def fidelity_matrix(fidelity_factor):
@@ -110,7 +135,7 @@
     own_first = (lax.axis_index("row") * lax.axis_size("col") + lax.axis_index("col")) * own_count
     all_embedding = lax.all_gather(embedding, ("row", "col"), axis=1, tiled=True)
     all_rung = lax.all_gather(rung_value, ("row", "col"), axis=0, tiled=True)
-    all_targets = lax.all_gather(targets, ("row", "col"), axis=1, tiled=True)
+    all_targets = _hold_streams(targets, ("row", "col"), where_dim=1)
     squares = jnp.sum(jnp.square(all_embedding.astype(jnp.float32)), axis=0)
     col_fidelity = rung_fidelity(fidelity, all_rung)
     solution = jnp.zeros_like(all_targets)

time: 122 us -> 118 us (0.967)
  blocking collectives: 60.5 us -> 40.8 us
  matrix products: 45.3 us -> 52.2 us
  waiting for transfers between devices: 0 us -> 5.15 us
  starting transfers between devices: 0 us -> 2.38 us
    all_gather x1 -> x0, blocking collectives: 19.3 us -> none  [on_device(): all_targets = lax.all_gather(targets, ('row', 'col'), axis=1, tiled=True)]
    ppermute x0 -> x4, waiting for transfers between devices: none -> 5.15 us  [watch_the_racks(): t_next = jax.lax.ppermute(oldest, axis_name=mesh_ax, perm=v1)]
    dot_general x3, matrix products: 9.19 us -> 13.1 us  [left_product(): lax.dot_general(weights, values, (((0,), (0,)), ((), ())), preferred_elem...]
    dot_general x2, matrix products: 31.2 us -> 34.4 us  [one_col_block(): lax.dot_general(cols_direction, kernel, (((1,), (1,)), ((), ())), precisi...]
    ppermute x0 -> x4, starting transfers between devices: none -> 2.38 us  [watch_the_racks(): t_next = jax.lax.ppermute(oldest, axis_name=mesh_ax, perm=v1)]
  transfers between devices with their start and end apart: 0 -> 4, of which waited for: 0 -> 2; matrix products, arithmetic and copies ran while one was open for 0% -> 13% of each run, Pallas kernels for 0% -> 0%
where the time goes in v1:
time: 118 us; the launch traced here: 117 us
  matrix products  52.2 us (44%)
  blocking collectives  40.8 us (35%)
  other arithmetic  14.3 us (12%)
  waiting for transfers between devices  5.15 us (4%)
  starting transfers between devices  2.38 us (2%)
  between operations  2.14 us (2%)
    dot_general x2, matrix products, one_col_block(): lax.dot_general(cols_direction, kernel, (((1,), (1,)), ((), ())), precisi...  34.4 us
    all_gather x1, blocking collectives, on_device(): all_rung = lax.all_gather(rung_value, ('row', 'col'), axis=0, tiled=True)  22.7 us
    all_gather x1, blocking collectives, on_device(): lax.all_gather(embedding, ('row', 'col'), axis=1, tiled=True)  18.2 us
    dot_general x3, matrix products, left_product(): lax.dot_general(weights, values, (((0,), (0,)), ((), ())), preferred_elem...  13.1 us
    another operation x9, other arithmetic, solve_spd(): jnp.linalg.cholesky(matrix)  6.51 us
    another operation x6, other arithmetic, solve_spd(): jax.scipy.linalg.cho_solve((jnp.linalg.cholesky(matrix), True), right_side)  5.63 us
    ppermute x4, waiting for transfers between devices, watch_the_racks(): t_next = jax.lax.ppermute(oldest, axis_name=mesh_ax, perm=v1)  5.15 us
    ppermute x4, starting transfers between devices, watch_the_racks(): t_next = jax.lax.ppermute(oldest, axis_name=mesh_ax, perm=v1)  2.38 us
  transfers between devices with their start and end apart: 4, of which 2 were waited for; matrix products, arithmetic and copies ran while one was open for 13% of the time, Pallas kernels for 0%

profile of v1, /device:TPU:0, one launch (start us, length us, event | category | flops | bytes accessed | tf_op | source)
XLA Modules:
  0.0 117.4 jit_solution(16731224381298234991)
XLA Ops:
  0.6 0.6 collective-permute-start
  1.2 0.7 convert_bitcast_fusion
  1.9 0.9 convolution_add_fusion.5
  2.7 22.7 %all-gather = bf16[16,1,128]{2,1,0:T(2,128)(2,1)S(1)} all-gather(bf16[1,1,128]{2,1,0:T(2,128)(2,1)S(1)} %convert_bitcast_fusion), channel_id=1, replica_groups=mesh['task'=2,'row'=4,'col'=4] {'row','col'}, dimensions={0}, use_global_device_ids=true | all-gather | bytes 4352 | tf_op jit(solution)/shard_map/all_gather | solution.py:137
  25.6 1.3 %multiply_convert_fusion.1 = bf16[512,128]{1,0:T(8,128)(2,1)S(1)} fusion(bf16[164,512]{1,0:T(8,128)(2,1)} %param.16, bf16[164,128]{1,0:T(8,128)(2,1)} %param.14, f32[512]{0:T(512)} %param.17), kind=kOutput, calls=%fused_computation.14 | convolution fusion | flops 21889024 | bytes 343040 | tf_op jit(solution)/shard_map/dot_general | solution.py:42
  26.9 1.3 %fusion.1 = bf16[64,128]{1,0:T(8,128)(2,1)S(1)} fusion(bf16[512,64]{0,1:T(8,128)(2,1)} %param.20, bf16[512,128]{1,0:T(8,128)(2,1)S(1)} %multiply_convert_fusion.1, bf16[512,512]{1,0:T(8,128)(2,1)S(1)} %copy-done, f32[512]{0:T(512)} %param.19), kind=kOutput, calls=%fused_computation.9 | convolution fusion | flops 75898880 | bytes 739328 | tf_op jit(solution)/shard_map/dot_general | solution.py:42
  28.3 18.2 %all_gather.6 = bf16[64,2048]{1,0:T(8,128)(2,1)S(1)} all-gather(bf16[64,128]{1,0:T(8,128)(2,1)S(1)} %fusion.1), channel_id=1, replica_groups=mesh['task'=2,'row'=4,'col'=4] {'row','col'}, dimensions={1}, use_global_device_ids=true | all-gather | bytes 278528 | tf_op jit(solution)/shard_map/all_gather | solution.py:136
  46.4 0.7 pad_maximum_fusion.3
  47.1 1.7 %collective-permute-start.1 = (f32[2,16,128]{2,1,0:T(8,128)S(1)}, f32[2,16,128]{2,1,0:T(8,128)S(1)}, u32[]{:S(2)}, u32[]{:S(2)}) collective-permute-start(f32[2,16,128]{2,1,0:T(8,128)S(1)} %get-tuple-element.137), channel_id=1, source_target_pairs={{0,2},{1,3},{2,0},{3,1},{4,6},{5,7},{6,4},{7,5},{8,10},{9,11},{10,... | collective-permute-start | bytes 49160 | tf_op jit(solution)/shard_map/ppermute | solution.py:21
  48.9 2.0 %collective-permute-done.1 = f32[2,16,128]{2,1,0:T(8,128)S(1)} collective-permute-done((f32[2,16,128]{2,1,0:T(8,128)S(1)}, f32[2,16,128]{2,1,0:T(8,128)S(1)}, u32[]{:S(2)}, u32[]{:S(2)}) %collective-permute-start.1) | collective-permute-done | bytes 16416 | tf_op jit(solution)/shard_map/ppermute | solution.py:21
  51.7 3.2 %collective-permute-done.2 = f32[4,16,128]{2,1,0:T(8,128)S(1)} collective-permute-done((f32[4,16,128]{2,1,0:T(8,128)S(1)}, f32[4,16,128]{2,1,0:T(8,128)S(1)}, u32[]{:S(2)}, u32[]{:S(2)}) %collective-permute-start.2) | collective-permute-done | bytes 32800 | tf_op jit(solution)/shard_map/ppermute | solution.py:21
  55.0 10.5 %select_multiply_fusion = f32[2048,2048]{1,0:T(8,128)} fusion(bf16[64,2048]{1,0:T(8,128)(2,1)S(1)} %all_gather.6, f32[2048]{0:T(1024)S(1)} %bitcast.136, f32[2048]{0:T(1024)S(1)} %bitcast.137, f32[2048]{0:T(1024)S(1)} %bitcast.138, f32[2048]{0:T(1024)S(1)} %bitcast.135, f32[2048]{0:T(1024)S(1)} %multiply_reduce_fusion, f32[]{:T(128)} %bitcast.14, ...), kind=kOutput, calls=%fused_computation | convolution fusion | flops 570425344 | bytes 17086468 | tf_op jit(solution)/shard_map/while/body/eval_jaxpr/while/body/eval_jaxpr/dot_general | solution.py:42
  66.5 17.2 %convolution_add_fusion.2 = f32[16,2048]{1,0:T(8,128)S(1)} fusion(f32[2048,2048]{1,0:T(8,128)} %select_multiply_fusion, f32[16,2,8,128]{3,2,1,0:T(8,128)S(1)} %bitcast.118, f32[]{:T(128)} %bitcast.115), kind=kOutput, calls=%fused_computation.4 | convolution fusion | flops 805371904 | bytes 17039364 | tf_op jit(solution)/shard_map/while/body/eval_jaxpr/while/body/eval_jaxpr/dot_general | solution.py:97
  84.0 1.5 %cholesky.59 = f32[16,16]{1,0:T(8,128)S(1)} custom-call(f32[16,16]{1,0:T(8,128)S(1)} %fusion.35), custom_call_target="Cholesky" | custom-call | tf_op jit(solution)/shard_map/jit(cholesky)/cholesky | solution.py:54
  85.5 0.6 compare_reduce_fusion.2
  86.2 0.6 fusion.18
  86.8 1.2 %custom-call.9 = f32[1,16,16]{1,2,0:T(8,128)S(1)} custom-call(f32[1,16,16]{2,1,0:T(8,128)S(1)} %fusion.18), custom_call_target="InvertDiagBlocksLowerTriangular" | custom-call | tf_op jit(solution)/shard_map/jit(_cho_solve)/triangular_solve | solution.py:54
  88.4 0.3 convolution_subtract_fusion
  88.8 0.3 fusion.3
  89.1 1.4 %cholesky.70 = f32[16,16]{1,0:T(8,128)S(1)} custom-call(f32[16,16]{1,0:T(8,128)S(1)} %fusion.30), custom_call_target="Cholesky" | custom-call | tf_op jit(solution)/shard_map/jit(cholesky)/cholesky | solution.py:54
  90.6 0.6 compare_reduce_fusion.1
  91.2 0.6 fusion.19
  91.9 1.2 %custom-call.10 = f32[1,16,16]{1,2,0:T(8,128)S(1)} custom-call(f32[1,16,16]{2,1,0:T(8,128)S(1)} %fusion.19), custom_call_target="InvertDiagBlocksLowerTriangular" | custom-call | tf_op jit(solution)/shard_map/jit(_cho_solve)/triangular_solve | solution.py:54
  93.7 0.3 convolution_add_fusion
  94.1 17.3 %convolution_add_fusion.1 = f32[16,2048]{1,0:T(8,128)S(1)} fusion(f32[16,2048]{1,0:T(8,128)S(1)} %convolution_add_fusion, f32[2048,2048]{1,0:T(8,128)} %select_multiply_fusion, f32[]{:T(128)} %bitcast.116), kind=kOutput, calls=%fused_computation.3 | convolution fusion | flops 805371904 | bytes 17039364 | tf_op jit(solution)/shard_map/while/body/eval_jaxpr/while/body/eval_jaxpr/dot_general | solution.py:97
  111.7 1.5 %cholesky.81 = f32[16,16]{1,0:T(8,128)S(1)} custom-call(f32[16,16]{1,0:T(8,128)S(1)} %fusion.25), custom_call_target="Cholesky" | custom-call | tf_op jit(solution)/shard_map/jit(cholesky)/cholesky | solution.py:54
  113.2 0.6 compare_reduce_fusion
  113.9 0.6 fusion.20
  114.5 1.2 %custom-call.11 = f32[1,16,16]{1,2,0:T(8,128)S(1)} custom-call(f32[1,16,16]{2,1,0:T(8,128)S(1)} %fusion.20), custom_call_target="InvertDiagBlocksLowerTriangular" | custom-call | tf_op jit(solution)/shard_map/jit(_cho_solve)/triangular_solve | solution.py:54
  116.1 0.3 fusion.44
  116.4 0.3 fusion.43
  116.8 0.6 dynamic-slice_subtract_fusion
  (38 shorter events, 3.0 us)
Async XLA Ops:
  0.6 26.3 %copy-start = (bf16[512,512]{1,0:T(8,128)(2,1)S(1)}, bf16[512,512]{1,0:T(8,128)(2,1)}, u32[]{:S(2)}) copy-start(bf16[512,512]{1,0:T(8,128)(2,1)} %param.18) | copy-start | bytes 1572868
  0.6 45.8 %collective-permute-start = (f32[1,16,128]{2,1,0:T(8,128)}, f32[1,16,128]{2,1,0:T(8,128)S(1)}, u32[]{:S(2)}, u32[]{:S(2)}) collective-permute-start(f32[1,16,128]{2,1,0:T(8,128)} %bitcast.132), channel_id=1, source_target_pairs={{0,1},{1,0},{2,3},{3,2},{4,5},{5,4},{6,7},{7,6},{8,9},{9,8},{10,11... | collective-permute-start | bytes 24584 | tf_op jit(solution)/shard_map/ppermute | solution.py:21
  47.1 3.7 %collective-permute-start.1 = (f32[2,16,128]{2,1,0:T(8,128)S(1)}, f32[2,16,128]{2,1,0:T(8,128)S(1)}, u32[]{:S(2)}, u32[]{:S(2)}) collective-permute-start(f32[2,16,128]{2,1,0:T(8,128)S(1)} %get-tuple-element.137), channel_id=1, source_target_pairs={{0,2},{1,3},{2,0},{3,1},{4,6},{5,7},{6,4},{7,5},{8,10},{9,11},{10,... | collective-permute-start | bytes 49160 | tf_op jit(solution)/shard_map/ppermute | solution.py:21
  50.9 4.0 %collective-permute-start.2 = (f32[4,16,128]{2,1,0:T(8,128)S(1)}, f32[4,16,128]{2,1,0:T(8,128)S(1)}, u32[]{:S(2)}, u32[]{:S(2)}) collective-permute-start(f32[4,16,128]{2,1,0:T(8,128)S(1)} %bitcast.125), channel_id=1, source_target_pairs={{0,4},{1,5},{2,6},{3,7},{4,0},{5,1},{6,2},{7,3},{8,12},{9,13},{10,... | collective-permute-start | bytes 98312 | tf_op jit(solution)/shard_map/ppermute | solution.py:21
  54.9 11.3 %collective-permute-start.3 = (f32[8,16,128]{2,1,0:T(8,128)S(1)}, f32[8,16,128]{2,1,0:T(8,128)S(1)}, u32[]{:S(2)}, u32[]{:S(2)}) collective-permute-start(f32[8,16,128]{2,1,0:T(8,128)S(1)} %bitcast.123), channel_id=1, source_target_pairs={{0,8},{1,9},{2,10},{3,11},{4,12},{5,13},{6,14},{7,15},{8,0},{9,1},... | collective-permute-start | bytes 196616 | tf_op jit(solution)/shard_map/ppermute | solution.py:21
